TPU v7x, 128 devices: a whole 4x4x4 slice. The times are simulated.
128 devices in a mesh: segment: 2 (over core), tensor: 4 (over x), batch: 16 (over z, y).
Axes of the slice: x: 4, y: 4, z: 4, core: 2. Of those that a mesh axis runs over, the one named last changes fastest.
Arguments:
- hidden: bfloat16 [3, 128, 16384], P(None, 'tensor', 'batch'), may hold values from -6 to 6
- norm_gain: bfloat16 [2, 16384], P('segment', 'batch'), may hold values from 0.25 to 1.75
- w_query: bfloat16 [2, 16384, 8192], P('segment', 'batch', 'tensor'), may hold values from -0.046875 to 0.046875
- key_value_weight: bfloat16 [2, 16384, 2048], P('segment', 'batch', 'tensor'), may hold values from -0.046875 to 0.046875
- w_out: bfloat16 [2, 8192, 16384], P('segment', 'tensor', 'batch'), may hold values from -0.0625 to 0.0625
- key_value_cache: bfloat16 [2, 32, 8, 256, 256], P('segment', 'batch', 'tensor'), may hold values from -6 to 6
- owner_slot: int32 [32], replicated, may hold values from 0 to 31, each once
- accepted: int32 [3, 32], replicated, may hold values from 1 to 4
Outputs:
- layer_outputs: bfloat16 [2, 3, 128, 16384], P('segment', None, 'tensor', 'batch')
- new_cache: bfloat16 [2, 32, 8, 12, 256], P('segment', 'batch', 'tensor')
Inputs may be any that keep to these rules, and one draw needn't show every extreme that they name: `owner_slot`: each slot is held by exactly one request; slot s belongs to index s // 2 of batch.
All inputs are finite; a program needn't handle non-finite values.
Results may differ from a plain program's by a relative error of at most 0.0095.
Values may be sent and summed in bfloat16 or wider, within the bound.
No kernel may reach another device: no remote copies, remote signals or barrier semaphores. Data moves between devices by JAX's collectives and lax.ppermute only.
A program may use at most 64 MiB of HBM per device.

v0:
```python
import jax
import jax.numpy as jnp
from jax import lax
from jax.sharding import PartitionSpec as P

MODEL_WIDTH = 16384
HEAD_SIZE = 128
DRAFT_BLOCK = 4
DECODE_ROUNDS = 3
GROUP_HEADS = 8


def passed_along(block, axis, distance):
    devices = range(lax.axis_size(axis))
    route = [(i - distance, i) for i in devices if i - distance in devices]
    return lax.ppermute(block, axis, route)


def pass_on(rows):
    return passed_along(rows, "segment", 1)


def shards(
    hidden, norm_gain, w_query, key_value_weight, w_out, key_value_cache, owner_slot, accepted
):
    n_segment = lax.axis_size("segment")
    segment = lax.axis_index("segment")
    group = lax.axis_index("batch")
    requests = owner_slot.shape[0]
    slots = key_value_cache.shape[1]
    kv_local = key_value_cache.shape[2]
    query_cols = w_query.shape[2]
    own_rows = slots * DRAFT_BLOCK
    scale = HEAD_SIZE ** (-0.5)
    gain = norm_gain[0].astype(jnp.float32)
    cache_local = key_value_cache[0]
    onehot = (owner_slot[None, :] == jnp.arange(requests)[:, None]).astype(jnp.int32)
    inverse = jnp.sum(onehot * jnp.arange(requests)[None, :], axis=1)
    acc_slot = jnp.sum(onehot[None] * accepted[:, None, :], axis=2)
    acc_own = lax.dynamic_slice_in_dim(acc_slot, group * slots, slots, 1)
    sort_index = (inverse[:, None] * DRAFT_BLOCK + jnp.arange(DRAFT_BLOCK)[None, :]).reshape(-1)
    back_index = (owner_slot[:, None] * DRAFT_BLOCK + jnp.arange(DRAFT_BLOCK)[None, :]).reshape(-1)
    positions = jnp.arange(DECODE_ROUNDS * DRAFT_BLOCK)
    round_of = positions // DRAFT_BLOCK
    place = positions % DRAFT_BLOCK
    causal = jnp.arange(DRAFT_BLOCK)[None, :] <= jnp.arange(DRAFT_BLOCK)[:, None]
    ext = jnp.zeros((slots, kv_local, DECODE_ROUNDS * DRAFT_BLOCK, 2 * HEAD_SIZE), jnp.bfloat16)
    record = jnp.zeros((DECODE_ROUNDS,) + hidden.shape[1:], jnp.bfloat16)
    x = jnp.zeros(hidden.shape[1:], jnp.bfloat16)
    for rnd in range(DECODE_ROUNDS):
        for step in range(n_segment):
            if step == 0:
                x = jnp.where(segment == 0, hidden[rnd], x)
            layer_rnd = jnp.int32(rnd)
            xf = x.astype(jnp.float32)
            total = lax.psum(jnp.sum(xf * xf, axis=1), "batch")
            normed = (xf * lax.rsqrt(total / MODEL_WIDTH + 1e-05)[:, None] * gain[None, :]).astype(
                jnp.bfloat16
            )
            rows_all = lax.all_gather(normed, "tensor", axis=0, tiled=True)
            sorted_rows = jnp.take(rows_all, sort_index, axis=0)
            first = jnp.dot(sorted_rows, w_query[0], preferred_element_type=jnp.float32)
            second = jnp.dot(sorted_rows, key_value_weight[0], preferred_element_type=jnp.float32)
            proj = lax.psum_scatter(
                jnp.concatenate([first, second], axis=1), "batch", scatter_dimension=0, tiled=True
            )
            query_rows_new = proj[:, :query_cols].astype(jnp.bfloat16)
            key_value_rows = proj[:, query_cols:].astype(jnp.bfloat16)
            query_heads = query_rows_new.reshape(
                slots, DRAFT_BLOCK, kv_local, GROUP_HEADS, HEAD_SIZE
            )
            fresh_key_value = key_value_rows.reshape(
                slots, DRAFT_BLOCK, kv_local, 2 * HEAD_SIZE
            ).transpose(0, 2, 1, 3)
            keys_all = jnp.concatenate([cache_local, ext, fresh_key_value], axis=2)
            acc_by_pos = acc_own[round_of, :].T
            ext_valid = (round_of[None, :] < layer_rnd) & (place[None, :] < acc_by_pos)
            mask = jnp.concatenate(
                [
                    jnp.ones((slots, DRAFT_BLOCK, cache_local.shape[2]), bool),
                    jnp.broadcast_to(
                        ext_valid[:, None, :], (slots, DRAFT_BLOCK, DECODE_ROUNDS * DRAFT_BLOCK)
                    ),
                    jnp.broadcast_to(causal[None], (slots, DRAFT_BLOCK, DRAFT_BLOCK)),
                ],
                axis=2,
            )
            scores = (
                jnp.einsum(
                    "sjhgd,shld->shgjl",
                    query_heads,
                    keys_all[..., :HEAD_SIZE],
                    preferred_element_type=jnp.float32,
                )
                * scale
            )
            scores = jnp.where(mask[:, None, None], scores, -1e30)
            weights = jax.nn.softmax(scores, axis=-1).astype(jnp.bfloat16)
            attended = jnp.einsum(
                "shgjl,shld->sjhgd",
                weights,
                keys_all[..., HEAD_SIZE:],
                preferred_element_type=jnp.float32,
            )
            attended = attended.astype(jnp.bfloat16).reshape(own_rows, query_cols)
            partial_out = jnp.dot(
                lax.all_gather(attended, "batch", axis=0, tiled=True),
                w_out[0],
                preferred_element_type=jnp.float32,
            )
            unsorted = jnp.take(partial_out, back_index, axis=0)
            summed = lax.psum_scatter(
                unsorted.astype(jnp.bfloat16), "tensor", scatter_dimension=0, tiled=True
            ).astype(jnp.float32)
            x_new = (xf + summed).astype(jnp.bfloat16)
            acc_now = lax.dynamic_index_in_dim(acc_own, layer_rnd, 0, keepdims=False)
            keep = jnp.arange(DRAFT_BLOCK)[None, :] < acc_now[:, None]
            masked = jnp.where(
                keep[:, None, :, None], fresh_key_value, jnp.zeros_like(fresh_key_value)
            )
            ext_new = lax.dynamic_update_slice(ext, masked, (0, 0, layer_rnd * DRAFT_BLOCK, 0))
            x_new, ext_new = (x_new, ext_new)
            active = segment == step
            ext = jnp.where(active, ext_new, ext)
            record = record.at[rnd].set(jnp.where(active, x_new, record[rnd]))
            if step + 1 < n_segment:
                x = pass_on(x_new)
    return (record[None], ext[None])


def solution(mesh):
    in_specs = (
        P(None, "tensor", "batch"),
        P("segment", "batch"),
        P("segment", "batch", "tensor"),
        P("segment", "batch", "tensor"),
        P("segment", "tensor", "batch"),
        P("segment", "batch", "tensor", None, None),
        P(),
        P(),
    )
    out_specs = (P("segment", None, "tensor", "batch"), P("segment", "batch", "tensor", None, None))
    return jax.shard_map(shards, mesh=mesh, in_specs=in_specs, out_specs=out_specs, check_vma=False)
```

profile of v0, /device:TPU:0, one launch (start us, length us, event | category | flops | bytes accessed | tf_op | source)
XLA Modules:
  0.0 944.5 jit_solution(7901623505001223784)
XLA Ops:
  10.1 1.3 fusion.120
  14.7 42.0 %psum.42 = f32[32]{0:T(128)S(1)} all-reduce(f32[32]{0:T(128)S(1)} %fusion.92), channel_id=1, replica_groups=mesh['segment'=2,'tensor'=4,'batch'=16] {'batch'}, use_global_device_ids=true, to_apply=%region_1.0 | all-reduce | flops 32 | bytes 256 | tf_op jit(solution)/shard_map/psum | solution.py:56
  57.7 12.6 %all_gather.36 = bf16[128,1024]{1,0:T(8,128)(2,1)S(1)} all-gather(bf16[32,1024]{1,0:T(8,128)(2,1)S(1)} %fusion.94), channel_id=1, replica_groups=mesh['segment'=2,'tensor'=4,'batch'=16] {'tensor'}, dimensions={0}, use_global_device_ids=true | all-gather | bytes 327680 | tf_op jit(solution)/shard_map/all_gather | solution.py:60
  71.5 3.0 fusion.28
  74.6 82.2 %all-reduce.16 = bf16[128,2560]{1,0:T(8,128)(2,1)S(1)} all-reduce(f32[128,2560]{1,0:T(8,128)S(1)} %pad_maximum_fusion), channel_id=2, replica_groups=mesh['segment'=2,'tensor'=4,'batch'=16] {'batch'}, use_global_device_ids=true, to_apply=%region_3.5.clone | all-reduce | flops 327680 | bytes 1966080
  156.8 1.2 dynamic-slice.57
  164.6 20.9 %all_gather.37 = bf16[128,2048]{1,0:T(8,128)(2,1)S(1)} all-gather(bf16[8,2048]{1,0:T(8,128)(2,1)S(1)} %reshape.476), channel_id=1, replica_groups=mesh['segment'=2,'tensor'=4,'batch'=16] {'batch'}, dimensions={0}, use_global_device_ids=true | all-gather | bytes 557056 | tf_op jit(solution)/shard_map/all_gather | solution.py:107
  185.6 2.9 fusion.16
  190.5 20.0 %reduce-scatter.7.cloned.1.call-done = bf16[32,1024]{1,0:T(8,128)(2,1)} async-done(((bf16[128,1024]{1,0:T(8,128)(2,1)}), bf16[32,1024]{1,0:T(8,128)(2,1)}) %reduce-scatter.7.cloned.1.call-update) | async-done | bytes 65552 | tf_op jit(solution)/shard_map/reduce_scatter | solution.py:112
  211.3 1.3 collective-permute-start
  213.6 40.6 %all-reduce.11 = (f32[32]{0:T(128)S(1)}, f32[32]{0:T(128)S(1)}) all-reduce(f32[32]{0:T(128)S(1)} %get-tuple-element.111, f32[32]{0:T(128)S(1)} %get-tuple-element.102), channel_id=1, replica_groups=mesh['segment'=2,'tensor'=4,'batch'=16] {'batch'}, use_global_device_ids=true, to_apply=%region_9.12 | all-reduce | flops 64 | bytes 512 | tf_op jit(solution)/shard_map/psum | solution.py:56
  254.3 12.4 %all_gather.38 = bf16[128,1024]{1,0:T(8,128)(2,1)S(1)} all-gather(bf16[32,1024]{1,0:T(8,128)(2,1)S(1)} %get-tuple-element.115), channel_id=1, replica_groups=mesh['segment'=2,'tensor'=4,'batch'=16] {'tensor'}, dimensions={0}, use_global_device_ids=true | all-gather | bytes 327680 | tf_op jit(solution)/shard_map/all_gather | solution.py:60
  267.9 4.0 fusion.26
  271.9 12.2 %all_gather.40 = bf16[128,1024]{1,0:T(8,128)(2,1)S(1)} all-gather(bf16[32,1024]{1,0:T(8,128)(2,1)S(1)} %get-tuple-element.114), channel_id=1, replica_groups=mesh['segment'=2,'tensor'=4,'batch'=16] {'tensor'}, dimensions={0}, use_global_device_ids=true | all-gather | bytes 327680 | tf_op jit(solution)/shard_map/all_gather | solution.py:60
  285.3 3.0 fusion.24
  288.5 1.2 pad_maximum_fusion.2
  289.7 88.6 %all-reduce.17 = (bf16[128,2560]{1,0:T(8,128)(2,1)}, bf16[128,2560]{1,0:T(8,128)(2,1)}) all-reduce(f32[128,2560]{1,0:T(8,128)S(1)} %pad_maximum_fusion.1, f32[128,2560]{1,0:T(8,128)} %pad_maximum_fusion.2), channel_id=4, replica_groups=mesh['segment'=2,'tensor'=4,'batch'=16] {'batch'}, use_global_device_ids=true, to_apply=%region_10.13.clone | all-reduce | flops 655360 | bytes 3932160
  381.4 1.3 fusion.56
  382.7 21.0 %all_gather.41 = bf16[128,2048]{1,0:T(8,128)(2,1)S(1)} all-gather(bf16[8,2048]{1,0:T(8,128)(2,1)S(1)} %reshape.483), channel_id=1, replica_groups=mesh['segment'=2,'tensor'=4,'batch'=16] {'batch'}, dimensions={0}, use_global_device_ids=true | all-gather | bytes 557056 | tf_op jit(solution)/shard_map/all_gather | solution.py:107
  403.7 2.9 fusion.12
  408.3 24.3 %all_gather.39 = bf16[128,2048]{1,0:T(8,128)(2,1)S(1)} all-gather(bf16[8,2048]{1,0:T(8,128)(2,1)S(1)} %reshape.479), channel_id=1, replica_groups=mesh['segment'=2,'tensor'=4,'batch'=16] {'batch'}, dimensions={0}, use_global_device_ids=true | all-gather | bytes 557056 | tf_op jit(solution)/shard_map/all_gather | solution.py:107
  432.5 3.0 fusion.14
  438.8 16.3 %reduce-scatter.9.cloned.1.call-done = bf16[32,1024]{1,0:T(8,128)(2,1)} async-done(((bf16[128,1024]{1,0:T(8,128)(2,1)}), bf16[32,1024]{1,0:T(8,128)(2,1)}) %reduce-scatter.9.cloned.1.call-update) | async-done | bytes 65552 | tf_op jit(solution)/shard_map/reduce_scatter | solution.py:112
  456.0 22.1 %reduce-scatter.11.cloned.1.call-done = bf16[32,1024]{1,0:T(8,128)(2,1)} async-done(((bf16[128,1024]{1,0:T(8,128)(2,1)}), bf16[32,1024]{1,0:T(8,128)(2,1)}) %reduce-scatter.11.cloned.1.call-update) | async-done | bytes 65552 | tf_op jit(solution)/shard_map/reduce_scatter | solution.py:112
  479.0 1.3 collective-permute-start.1
  482.1 40.6 %all-reduce.9 = (f32[32]{0:T(128)S(1)}, f32[32]{0:T(128)S(1)}) all-reduce(f32[32]{0:T(128)S(1)} %get-tuple-element.110, f32[32]{0:T(128)S(1)} %get-tuple-element.98), channel_id=1, replica_groups=mesh['segment'=2,'tensor'=4,'batch'=16] {'batch'}, use_global_device_ids=true, to_apply=%region_21.24 | all-reduce | flops 64 | bytes 512 | tf_op jit(solution)/shard_map/psum | solution.py:56
  522.9 12.3 %all_gather.42 = bf16[128,1024]{1,0:T(8,128)(2,1)S(1)} all-gather(bf16[32,1024]{1,0:T(8,128)(2,1)S(1)} %get-tuple-element.113), channel_id=1, replica_groups=mesh['segment'=2,'tensor'=4,'batch'=16] {'tensor'}, dimensions={0}, use_global_device_ids=true | all-gather | bytes 327680 | tf_op jit(solution)/shard_map/all_gather | solution.py:60
  536.5 4.0 fusion.22
  540.4 12.2 %all_gather.44 = bf16[128,1024]{1,0:T(8,128)(2,1)S(1)} all-gather(bf16[32,1024]{1,0:T(8,128)(2,1)S(1)} %get-tuple-element.112), channel_id=1, replica_groups=mesh['segment'=2,'tensor'=4,'batch'=16] {'tensor'}, dimensions={0}, use_global_device_ids=true | all-gather | bytes 327680 | tf_op jit(solution)/shard_map/all_gather | solution.py:60
  554.0 3.0 fusion.20
  557.2 1.2 pad_maximum_fusion.4
  558.3 88.6 %all-reduce.18 = (bf16[128,2560]{1,0:T(8,128)(2,1)}, bf16[128,2560]{1,0:T(8,128)(2,1)}) all-reduce(f32[128,2560]{1,0:T(8,128)S(1)} %pad_maximum_fusion.3, f32[128,2560]{1,0:T(8,128)} %pad_maximum_fusion.4), channel_id=8, replica_groups=mesh['segment'=2,'tensor'=4,'batch'=16] {'batch'}, use_global_device_ids=true, to_apply=%region_22.25.clone | all-reduce | flops 655360 | bytes 3932160
  650.1 1.3 fusion.58
  651.4 21.0 %all_gather.45 = bf16[128,2048]{1,0:T(8,128)(2,1)S(1)} all-gather(bf16[8,2048]{1,0:T(8,128)(2,1)S(1)} %reshape.490), channel_id=1, replica_groups=mesh['segment'=2,'tensor'=4,'batch'=16] {'batch'}, dimensions={0}, use_global_device_ids=true | all-gather | bytes 557056 | tf_op jit(solution)/shard_map/all_gather | solution.py:107
  672.4 3.0 fusion.8
  677.1 24.1 %all_gather.43 = bf16[128,2048]{1,0:T(8,128)(2,1)S(1)} all-gather(bf16[8,2048]{1,0:T(8,128)(2,1)S(1)} %reshape.486), channel_id=1, replica_groups=mesh['segment'=2,'tensor'=4,'batch'=16] {'batch'}, dimensions={0}, use_global_device_ids=true | all-gather | bytes 557056 | tf_op jit(solution)/shard_map/all_gather | solution.py:107
  701.2 3.0 fusion.10
  706.8 17.1 %reduce-scatter.13.cloned.1.call-done = bf16[32,1024]{1,0:T(8,128)(2,1)} async-done(((bf16[128,1024]{1,0:T(8,128)(2,1)}), bf16[32,1024]{1,0:T(8,128)(2,1)}) %reduce-scatter.13.cloned.1.call-update) | async-done | bytes 65552 | tf_op jit(solution)/shard_map/reduce_scatter | solution.py:112
  724.9 21.9 %reduce-scatter.15.cloned.1.call-done = bf16[32,1024]{1,0:T(8,128)(2,1)} async-done(((bf16[128,1024]{1,0:T(8,128)(2,1)}), bf16[32,1024]{1,0:T(8,128)(2,1)}) %reduce-scatter.15.cloned.1.call-update) | async-done | bytes 65552 | tf_op jit(solution)/shard_map/reduce_scatter | solution.py:112
  747.6 1.3 collective-permute-start.2
  749.9 40.5 %psum.47 = f32[32]{0:T(128)S(1)} all-reduce(f32[32]{0:T(128)S(1)} %fusion.88), channel_id=1, replica_groups=mesh['segment'=2,'tensor'=4,'batch'=16] {'batch'}, use_global_device_ids=true, to_apply=%region_33.36 | all-reduce | flops 32 | bytes 256 | tf_op jit(solution)/shard_map/psum | solution.py:56
  790.6 12.3 %all_gather.46 = bf16[128,1024]{1,0:T(8,128)(2,1)S(1)} all-gather(bf16[32,1024]{1,0:T(8,128)(2,1)S(1)} %fusion.90), channel_id=1, replica_groups=mesh['segment'=2,'tensor'=4,'batch'=16] {'tensor'}, dimensions={0}, use_global_device_ids=true | all-gather | bytes 327680 | tf_op jit(solution)/shard_map/all_gather | solution.py:60
  804.2 2.9 fusion.18
  807.3 82.3 %all-reduce.19 = bf16[128,2560]{1,0:T(8,128)(2,1)} all-reduce(f32[128,2560]{1,0:T(8,128)S(1)} %pad_maximum_fusion.5), channel_id=12, replica_groups=mesh['segment'=2,'tensor'=4,'batch'=16] {'batch'}, use_global_device_ids=true, to_apply=%region_34.37.clone | all-reduce | flops 327680 | bytes 1966080
  891.2 20.9 %all_gather.47 = bf16[128,2048]{1,0:T(8,128)(2,1)S(1)} all-gather(bf16[8,2048]{1,0:T(8,128)(2,1)S(1)} %reshape.493), channel_id=1, replica_groups=mesh['segment'=2,'tensor'=4,'batch'=16] {'batch'}, dimensions={0}, use_global_device_ids=true | all-gather | bytes 557056 | tf_op jit(solution)/shard_map/all_gather | solution.py:107
  912.2 2.9 fusion.6
  917.7 18.5 %reduce-scatter.17.cloned.1.call-done = bf16[32,1024]{1,0:T(8,128)(2,1)} async-done(((bf16[128,1024]{1,0:T(8,128)(2,1)}), bf16[32,1024]{1,0:T(8,128)(2,1)}) %reduce-scatter.17.cloned.1.call-update) | async-done | bytes 65552 | tf_op jit(solution)/shard_map/reduce_scatter | solution.py:112
  936.2 1.5 fusion.104
  (234 shorter events, 50.8 us)
Async XLA Ops:
  7.2 64.0 %copy-start = (bf16[1,1024,512]{2,1,0:T(8,128)(2,1)S(1)}, bf16[1,1024,512]{2,1,0:T(8,128)(2,1)}, u32[]{:S(2)}) copy-start(bf16[1,1024,512]{2,1,0:T(8,128)(2,1)} %param.27) | copy-start | bytes 3145732
  7.2 203.3 %reduce-scatter.7.cloned.1.call-start = ((), (), s32[]{:S(2)}) async-start(), calls=%async_computation.6 | async-start | bytes 327680 | tf_op jit(solution)/shard_map/reduce_scatter | solution.py:112
  70.3 213.8 %copy-start.16 = (s32[1024]{0:T(1024)}, s32[1024]{0:T(1024)S(1)}, u32[]{:S(2)}) copy-start(s32[1024]{0:T(1024)S(1)} %pad_clamp_fusion.2) | copy-start | bytes 12292
  74.6 88.5 %copy-start.1 = (bf16[1,2,2,256,256]{4,3,2,1,0:T(8,128)(2,1)S(1)}, bf16[1,2,2,256,256]{4,3,2,1,0:T(8,128)(2,1)}, u32[]{:S(2)}) copy-start(bf16[1,2,2,256,256]{4,3,2,1,0:T(8,128)(2,1)} %param.29) | copy-start | bytes 1572868
  156.8 6.3 copy-start.26
  158.9 277.4 %copy-start.18 = (pred[128]{0:T(512)(128)(4,1)}, pred[128]{0:T(512)(128)(4,1)S(1)}, u32[]{:S(2)}) copy-start(pred[128]{0:T(512)(128)(4,1)S(1)} %compare_and_fusion) | copy-start | bytes 388
  163.8 216.3 %copy-start.24 = (pred[2,4,272]{2,1,0:T(4,128)(4,1)}, pred[2,4,272]{2,1,0:T(4,128)(4,1)S(1)}, u32[]{:S(2)}) copy-start(pred[2,4,272]{2,1,0:T(4,128)(4,1)S(1)} %get-tuple-element.122) | copy-start | bytes 6532
  185.6 249.9 %copy-start.17 = (s32[1024]{0:T(1024)}, s32[1024]{0:T(1024)S(1)}, u32[]{:S(2)}) copy-start(s32[1024]{0:T(1024)S(1)} %pad_clamp_fusion) | copy-start | bytes 12292
  188.5 21.9 %copy-start.6 = (bf16[3,32,1024]{2,1,0:T(8,128)(2,1)S(1)}, bf16[3,32,1024]{2,1,0:T(8,128)(2,1)}, u32[]{:S(2)}) copy-start(bf16[3,32,1024]{2,1,0:T(8,128)(2,1)} %param.24) | copy-start | bytes 589828
  190.2 264.9 %reduce-scatter.9.cloned.1.call-start = ((), (), s32[]{:S(2)}) async-start(), calls=%async_computation.7 | async-start | bytes 327680 | tf_op jit(solution)/shard_map/reduce_scatter | solution.py:112
  211.3 2.2 collective-permute-start
  212.6 54.9 %copy-start.7 = (bf16[2,2,12,256]{3,2,1,0:T(8,128)(2,1)}, bf16[2,2,12,256]{3,2,1,0:T(8,128)(2,1)S(1)}, u32[]{:S(2)}) copy-start(bf16[2,2,12,256]{3,2,1,0:T(8,128)(2,1)S(1)} %pad_select_fusion) | copy-start | bytes 73732
  285.3 3.0 copy-start.2
  289.7 90.3 %copy-start.11 = (bf16[2,2,12,256]{3,2,1,0:T(8,128)(2,1)S(1)}, bf16[2,2,12,256]{3,2,1,0:T(8,128)(2,1)}, u32[]{:S(2)}) copy-start(bf16[2,2,12,256]{3,2,1,0:T(8,128)(2,1)} %copy-done.7) | copy-start | bytes 73732
  289.7 90.4 %copy-start.8 = (bf16[2,2,12,256]{3,2,1,0:T(8,128)(2,1)S(1)}, bf16[2,2,12,256]{3,2,1,0:T(8,128)(2,1)}, u32[]{:S(2)}) copy-start(bf16[2,2,12,256]{3,2,1,0:T(8,128)(2,1)} %copy-done.7) | copy-start | bytes 73732
  380.0 58.8 %copy-start.9 = (bf16[2,2,12,256]{3,2,1,0:T(8,128)(2,1)}, bf16[2,2,12,256]{3,2,1,0:T(8,128)(2,1)S(1)}, u32[]{:S(2)}) copy-start(bf16[2,2,12,256]{3,2,1,0:T(8,128)(2,1)S(1)} %fusion.121) | copy-start | bytes 73732
  380.1 0.8 copy-start.5
  437.3 40.8 %reduce-scatter.11.cloned.1.call-start = ((), (), s32[]{:S(2)}) async-start(), calls=%async_computation.8 | async-start | bytes 327680 | tf_op jit(solution)/shard_map/reduce_scatter | solution.py:112
  438.1 285.9 %reduce-scatter.13.cloned.1.call-start = ((), (), s32[]{:S(2)}) async-start(), calls=%async_computation.9 | async-start | bytes 327680 | tf_op jit(solution)/shard_map/reduce_scatter | solution.py:112
  438.8 96.3 %copy-start.21 = (pred[2,4]{1,0:T(4,128)(4,1)}, pred[2,4]{1,0:T(4,128)(4,1)S(1)}, u32[]{:S(2)}) copy-start(pred[2,4]{1,0:T(4,128)(4,1)S(1)} %get-tuple-element.133) | copy-start | bytes 28
  479.0 2.2 collective-permute-start.1
  480.4 54.8 %copy-start.13 = (bf16[2,2,12,256]{3,2,1,0:T(8,128)(2,1)}, bf16[2,2,12,256]{3,2,1,0:T(8,128)(2,1)S(1)}, u32[]{:S(2)}) copy-start(bf16[2,2,12,256]{3,2,1,0:T(8,128)(2,1)S(1)} %constant_dynamic-update-slice_fusion.1) | copy-start | bytes 73732
  554.0 3.0 copy-start.3
  558.3 90.3 %copy-start.10 = (bf16[2,2,12,256]{3,2,1,0:T(8,128)(2,1)S(1)}, bf16[2,2,12,256]{3,2,1,0:T(8,128)(2,1)}, u32[]{:S(2)}) copy-start(bf16[2,2,12,256]{3,2,1,0:T(8,128)(2,1)} %copy-done.9) | copy-start | bytes 73732
  558.3 90.3 %copy-start.12 = (bf16[2,2,12,256]{3,2,1,0:T(8,128)(2,1)S(1)}, bf16[2,2,12,256]{3,2,1,0:T(8,128)(2,1)}, u32[]{:S(2)}) copy-start(bf16[2,2,12,256]{3,2,1,0:T(8,128)(2,1)} %copy.173) | copy-start | bytes 73732
  558.3 90.3 %copy-start.22 = (pred[2,4]{1,0:T(4,128)(4,1)S(1)}, pred[2,4]{1,0:T(4,128)(4,1)}, u32[]{:S(2)}) copy-start(pred[2,4]{1,0:T(4,128)(4,1)} %copy-done.21) | copy-start | bytes 28
  558.3 90.4 %copy-start.14 = (bf16[2,2,12,256]{3,2,1,0:T(8,128)(2,1)S(1)}, bf16[2,2,12,256]{3,2,1,0:T(8,128)(2,1)}, u32[]{:S(2)}) copy-start(bf16[2,2,12,256]{3,2,1,0:T(8,128)(2,1)} %copy-done.13) | copy-start | bytes 73732
  647.0 2.7 copy-start.23
  648.8 0.8 copy-start.4
  675.3 1.0 copy-start.25
  704.2 1.0 copy-start.19
  705.2 43.8 %copy-start.20 = (pred[2,4]{1,0:T(4,128)(4,1)S(1)}, pred[2,4]{1,0:T(4,128)(4,1)}, u32[]{:S(2)}) copy-start(pred[2,4]{1,0:T(4,128)(4,1)} %get-tuple-element.132) | copy-start | bytes 28
  706.2 40.6 %reduce-scatter.15.cloned.1.call-start = ((), (), s32[]{:S(2)}) async-start(), calls=%async_computation.10 | async-start | bytes 327680 | tf_op jit(solution)/shard_map/reduce_scatter | solution.py:112
  706.8 229.4 %reduce-scatter.17.cloned.1.call-start = ((), (), s32[]{:S(2)}) async-start(), calls=%async_computation.11 | async-start | bytes 327680 | tf_op jit(solution)/shard_map/reduce_scatter | solution.py:112
  747.6 42.9 %copy-start.15 = (bf16[1,3,32,1024]{3,2,1,0:T(8,128)(2,1)}, bf16[1,3,32,1024]{3,2,1,0:T(8,128)(2,1)S(1)}, u32[]{:S(2)}) copy-start(bf16[1,3,32,1024]{3,2,1,0:T(8,128)(2,1)S(1)} %get-tuple-element.94) | copy-start | bytes 589828
  747.6 2.2 collective-permute-start.2
Sparse Core Ops, SparseCore 0:
  190.4 20.0 reduce-scatter.6
  437.5 17.6 reduce-scatter.8
  457.5 20.5 reduce-scatter.10
  706.3 17.6 reduce-scatter.12
  726.2 20.5 reduce-scatter.14
  917.1 19.0 reduce-scatter.16
where the time goes:
time: 947 us; the launch traced here: 945 us
  blocking collectives  712 us (75%)
  waiting for transfers between devices  119 us (13%)
  matrix products  44.8 us (5%)
  other arithmetic  28.4 us (3%)
  local copies, waits for them, and re-layouts  20.8 us (2%)
  between operations  15.8 us (2%)
    unnamed x4, blocking collectives  342 us
    psum x4, blocking collectives, shards(): total = lax.psum(jnp.sum(xf * xf, axis=1), 'batch')  164 us
    all_gather x6, blocking collectives, shards(): lax.all_gather(attended, 'batch', axis=0, tiled=True)  132 us
    reduce_scatter x6, waiting for transfers between devices, shards(): lax.psum_scatter(unsorted.astype(jnp.bfloat16), 'tensor', scatter_dimensi...  116 us
    all_gather x6, blocking collectives, shards(): rows_all = lax.all_gather(normed, 'tensor', axis=0, tiled=True)  74 us
    dot_general x6, matrix products, shards(): first = jnp.dot(sorted_rows, w_query[0], preferred_element_type=jnp.float32)  19.9 us
  transfers between devices with their start and end apart: 9, of which 9 were waited for; matrix products, arithmetic and copies ran while one was open for 0% of the time, Pallas kernels for 0%

commit v1 on v0

--- a/solution.py
+++ b/solution.py
@@ -8,6 +8,28 @@
 DRAFT_BLOCK = 4
 DECODE_ROUNDS = 3
 GROUP_HEADS = 8
+
+
+def laid_out(parts, dim):
+    lengths = list(parts.shape[1:])
+    lengths[dim] *= parts.shape[0]
+    return jnp.moveaxis(parts, 0, dim).reshape(lengths)
+
+
+def collect(shard, axis, dim):
+    count = lax.axis_size(axis)
+    pairs = [(i, (i + 1) % count) for i in range(count)]
+    back = [(b, a) for a, b in pairs]
+    lower, upper = ([], [])
+    for lap in range(count - 1):
+        if lap % 2 == 0:
+            lower.append(lax.ppermute(lower[-1] if lower else shard, axis, pairs))
+        else:
+            upper.append(lax.ppermute(upper[-1] if upper else shard, axis, back))
+    pieces = jnp.stack([*lower[::-1], shard, *upper])
+    shift = lax.axis_index(axis) - len(lower)
+    pieces = pieces[(jnp.arange(count) - shift) % count]
+    return laid_out(pieces, dim)
 
 
 def passed_along(block, axis, distance):
@@ -104,9 +126,7 @@
             )
             attended = attended.astype(jnp.bfloat16).reshape(own_rows, query_cols)
             partial_out = jnp.dot(
-                lax.all_gather(attended, "batch", axis=0, tiled=True),
-                w_out[0],
-                preferred_element_type=jnp.float32,
+                collect(attended, "batch", 0), w_out[0], preferred_element_type=jnp.float32
             )
             unsorted = jnp.take(partial_out, back_index, axis=0)
             summed = lax.psum_scatter(

time: 947 us -> 1080 us (1.14)
  starting transfers between devices: 4.12 us -> 185 us
  blocking collectives: 712 us -> 579 us
  waiting for transfers between devices: 119 us -> 179 us
  local copies, waits for them, and re-layouts: 20.8 us -> 37.8 us
    ppermute x0 -> x90, starting transfers between devices: none -> 181 us  [the longest x42 157 us: collect(): upper.append(lax.ppermute(upper[-1] if upper else shard, axis, back))]
    all_gather x6 -> x0, blocking collectives: 132 us -> none  [shards(): lax.all_gather(attended, 'batch', axis=0, tiled=True)]
    ppermute x0 -> x90, waiting for transfers between devices: none -> 62.5 us  [the longest x48 62.3 us: collect(): lower.append(lax.ppermute(lower[-1] if lower else shard, axis, pairs))]
  transfers between devices with their start and end apart: 9 -> 99, of which waited for: 9 -> 30; matrix products, arithmetic and copies ran while one was open for 0% -> 3% of each run, Pallas kernels for 0% -> 0%
where the time goes in v1:
time: 1080 us; the launch traced here: 1070 us
  blocking collectives  579 us (54%)
  starting transfers between devices  185 us (17%)
  waiting for transfers between devices  179 us (17%)
  matrix products  42.7 us (4%)
  local copies, waits for them, and re-layouts  37.8 us (3%)
  other arithmetic  29.1 us (3%)
  between operations  17 us (2%)
    unnamed x4, blocking collectives  341 us
    psum x4, blocking collectives, shards(): total = lax.psum(jnp.sum(xf * xf, axis=1), 'batch')  164 us
    ppermute x42, starting transfers between devices, collect(): upper.append(lax.ppermute(upper[-1] if upper else shard, axis, back))  157 us
    reduce_scatter x6, waiting for transfers between devices, shards(): lax.psum_scatter(unsorted.astype(jnp.bfloat16), 'tensor', scatter_dimensi...  113 us
    all_gather x6, blocking collectives, shards(): rows_all = lax.all_gather(normed, 'tensor', axis=0, tiled=True)  74.1 us
    ppermute x48, waiting for transfers between devices, collect(): lower.append(lax.ppermute(lower[-1] if lower else shard, axis, pairs))  62.3 us
    ppermute x48, starting transfers between devices, collect(): lower.append(lax.ppermute(lower[-1] if lower else shard, axis, pairs))  23.7 us
  transfers between devices with their start and end apart: 99, of which 30 were waited for; matrix products, arithmetic and copies ran while one was open for 3% of the time, Pallas kernels for 0%

profile of v1, /device:TPU:0, one launch (start us, length us, event | category | flops | bytes accessed | tf_op | source)
XLA Modules:
  0.0 1070.1 jit_solution(11097109121845150013)
XLA Ops:
  14.6 42.0 %psum.42 = f32[32]{0:T(128)S(1)} all-reduce(f32[32]{0:T(128)S(1)} %fusion.98), channel_id=1, replica_groups=mesh['segment'=2,'tensor'=4,'batch'=16] {'batch'}, use_global_device_ids=true, to_apply=%region_1.0 | all-reduce | flops 32 | bytes 256 | tf_op jit(solution)/shard_map/psum | solution.py:78
  57.6 12.6 %all_gather.18 = bf16[128,1024]{1,0:T(8,128)(2,1)S(1)} all-gather(bf16[32,1024]{1,0:T(8,128)(2,1)S(1)} %fusion.100), channel_id=1, replica_groups=mesh['segment'=2,'tensor'=4,'batch'=16] {'tensor'}, dimensions={0}, use_global_device_ids=true | all-gather | bytes 327680 | tf_op jit(solution)/shard_map/all_gather | solution.py:82
  74.5 82.1 %all-reduce.16 = bf16[128,2560]{1,0:T(8,128)(2,1)S(1)} all-reduce(f32[128,2560]{1,0:T(8,128)S(1)} %pad_maximum_fusion), channel_id=2, replica_groups=mesh['segment'=2,'tensor'=4,'batch'=16] {'batch'}, use_global_device_ids=true, to_apply=%region_3.5.clone | all-reduce | flops 327680 | bytes 1966080
  163.7 7.2 collective-permute-done
  170.9 5.3 collective-permute-start.8
  178.3 5.4 collective-permute-start.9
  185.4 5.6 collective-permute-start.10
  192.6 5.6 collective-permute-start.11
  199.9 5.6 collective-permute-start.12
  207.1 5.6 collective-permute-start.13
  214.4 5.5 collective-permute-start.14
  227.8 20.6 %reduce-scatter.7.cloned.1.call-done = bf16[32,1024]{1,0:T(8,128)(2,1)} async-done(((bf16[128,1024]{1,0:T(8,128)(2,1)}), bf16[32,1024]{1,0:T(8,128)(2,1)}) %reduce-scatter.7.cloned.1.call-update) | async-done | bytes 65552 | tf_op jit(solution)/shard_map/reduce_scatter | solution.py:132
  251.7 40.6 %all-reduce.11 = (f32[32]{0:T(128)S(1)}, f32[32]{0:T(128)S(1)}) all-reduce(f32[32]{0:T(128)S(1)} %get-tuple-element.111, f32[32]{0:T(128)S(1)} %get-tuple-element.102), channel_id=1, replica_groups=mesh['segment'=2,'tensor'=4,'batch'=16] {'batch'}, use_global_device_ids=true, to_apply=%region_9.12 | all-reduce | flops 64 | bytes 512 | tf_op jit(solution)/shard_map/psum | solution.py:78
  292.3 12.5 %all_gather.19 = bf16[128,1024]{1,0:T(8,128)(2,1)S(1)} all-gather(bf16[32,1024]{1,0:T(8,128)(2,1)S(1)} %get-tuple-element.115), channel_id=1, replica_groups=mesh['segment'=2,'tensor'=4,'batch'=16] {'tensor'}, dimensions={0}, use_global_device_ids=true | all-gather | bytes 327680 | tf_op jit(solution)/shard_map/all_gather | solution.py:82
  310.1 12.2 %all_gather.20 = bf16[128,1024]{1,0:T(8,128)(2,1)S(1)} all-gather(bf16[32,1024]{1,0:T(8,128)(2,1)S(1)} %get-tuple-element.114), channel_id=1, replica_groups=mesh['segment'=2,'tensor'=4,'batch'=16] {'tensor'}, dimensions={0}, use_global_device_ids=true | all-gather | bytes 327680 | tf_op jit(solution)/shard_map/all_gather | solution.py:82
  327.9 88.9 %all-reduce.17 = (bf16[128,2560]{1,0:T(8,128)(2,1)}, bf16[128,2560]{1,0:T(8,128)(2,1)}) all-reduce(f32[128,2560]{1,0:T(8,128)S(1)} %pad_maximum_fusion.1, f32[128,2560]{1,0:T(8,128)} %pad_maximum_fusion.2), channel_id=4, replica_groups=mesh['segment'=2,'tensor'=4,'batch'=16] {'batch'}, use_global_device_ids=true, to_apply=%region_10.13.clone | all-reduce | flops 655360 | bytes 3932160
  420.4 6.4 collective-permute-done.31
  426.8 5.3 collective-permute-start.39
  434.3 5.5 collective-permute-start.40
  441.9 5.3 collective-permute-start.41
  449.3 5.3 collective-permute-start.42
  471.7 5.3 collective-permute-start.45
  502.3 14.3 %reduce-scatter.9.cloned.1.call-done = bf16[32,1024]{1,0:T(8,128)(2,1)} async-done(((bf16[128,1024]{1,0:T(8,128)(2,1)}), bf16[32,1024]{1,0:T(8,128)(2,1)}) %reduce-scatter.9.cloned.1.call-update) | async-done | bytes 65552 | tf_op jit(solution)/shard_map/reduce_scatter | solution.py:132
  517.5 22.1 %reduce-scatter.11.cloned.1.call-done = bf16[32,1024]{1,0:T(8,128)(2,1)} async-done(((bf16[128,1024]{1,0:T(8,128)(2,1)}), bf16[32,1024]{1,0:T(8,128)(2,1)}) %reduce-scatter.11.cloned.1.call-update) | async-done | bytes 65552 | tf_op jit(solution)/shard_map/reduce_scatter | solution.py:132
  543.6 40.6 %all-reduce.9 = (f32[32]{0:T(128)S(1)}, f32[32]{0:T(128)S(1)}) all-reduce(f32[32]{0:T(128)S(1)} %get-tuple-element.110, f32[32]{0:T(128)S(1)} %get-tuple-element.98), channel_id=1, replica_groups=mesh['segment'=2,'tensor'=4,'batch'=16] {'batch'}, use_global_device_ids=true, to_apply=%region_21.24 | all-reduce | flops 64 | bytes 512 | tf_op jit(solution)/shard_map/psum | solution.py:78
  584.3 12.3 %all_gather.21 = bf16[128,1024]{1,0:T(8,128)(2,1)S(1)} all-gather(bf16[32,1024]{1,0:T(8,128)(2,1)S(1)} %get-tuple-element.113), channel_id=1, replica_groups=mesh['segment'=2,'tensor'=4,'batch'=16] {'tensor'}, dimensions={0}, use_global_device_ids=true | all-gather | bytes 327680 | tf_op jit(solution)/shard_map/all_gather | solution.py:82
  601.9 12.2 %all_gather.22 = bf16[128,1024]{1,0:T(8,128)(2,1)S(1)} all-gather(bf16[32,1024]{1,0:T(8,128)(2,1)S(1)} %get-tuple-element.112), channel_id=1, replica_groups=mesh['segment'=2,'tensor'=4,'batch'=16] {'tensor'}, dimensions={0}, use_global_device_ids=true | all-gather | bytes 327680 | tf_op jit(solution)/shard_map/all_gather | solution.py:82
  619.8 88.3 %all-reduce.18 = (bf16[128,2560]{1,0:T(8,128)(2,1)}, bf16[128,2560]{1,0:T(8,128)(2,1)}) all-reduce(f32[128,2560]{1,0:T(8,128)S(1)} %pad_maximum_fusion.3, f32[128,2560]{1,0:T(8,128)} %pad_maximum_fusion.4), channel_id=8, replica_groups=mesh['segment'=2,'tensor'=4,'batch'=16] {'batch'}, use_global_device_ids=true, to_apply=%region_22.25.clone | all-reduce | flops 655360 | bytes 3932160
  713.1 6.3 collective-permute-done.62
  719.4 5.8 collective-permute-start.70
  727.3 5.3 collective-permute-start.71
  734.7 5.4 collective-permute-start.72
  742.3 5.3 collective-permute-start.73
  764.5 5.3 collective-permute-start.76
  795.1 15.0 %reduce-scatter.13.cloned.1.call-done = bf16[32,1024]{1,0:T(8,128)(2,1)} async-done(((bf16[128,1024]{1,0:T(8,128)(2,1)}), bf16[32,1024]{1,0:T(8,128)(2,1)}) %reduce-scatter.13.cloned.1.call-update) | async-done | bytes 65552 | tf_op jit(solution)/shard_map/reduce_scatter | solution.py:132
  811.0 21.9 %reduce-scatter.15.cloned.1.call-done = bf16[32,1024]{1,0:T(8,128)(2,1)} async-done(((bf16[128,1024]{1,0:T(8,128)(2,1)}), bf16[32,1024]{1,0:T(8,128)(2,1)}) %reduce-scatter.15.cloned.1.call-update) | async-done | bytes 65552 | tf_op jit(solution)/shard_map/reduce_scatter | solution.py:132
  836.0 40.6 %psum.47 = f32[32]{0:T(128)S(1)} all-reduce(f32[32]{0:T(128)S(1)} %fusion.94), channel_id=1, replica_groups=mesh['segment'=2,'tensor'=4,'batch'=16] {'batch'}, use_global_device_ids=true, to_apply=%region_33.36 | all-reduce | flops 32 | bytes 256 | tf_op jit(solution)/shard_map/psum | solution.py:78
  876.7 12.3 %all_gather.23 = bf16[128,1024]{1,0:T(8,128)(2,1)S(1)} all-gather(bf16[32,1024]{1,0:T(8,128)(2,1)S(1)} %fusion.96), channel_id=1, replica_groups=mesh['segment'=2,'tensor'=4,'batch'=16] {'tensor'}, dimensions={0}, use_global_device_ids=true | all-gather | bytes 327680 | tf_op jit(solution)/shard_map/all_gather | solution.py:82
  893.4 82.2 %all-reduce.19 = bf16[128,2560]{1,0:T(8,128)(2,1)} all-reduce(f32[128,2560]{1,0:T(8,128)S(1)} %pad_maximum_fusion.5), channel_id=12, replica_groups=mesh['segment'=2,'tensor'=4,'batch'=16] {'batch'}, use_global_device_ids=true, to_apply=%region_34.37.clone | all-reduce | flops 327680 | bytes 1966080
  977.3 7.6 collective-permute-done.78
  984.9 5.3 collective-permute-start.86
  992.1 5.3 collective-permute-start.87
  999.4 5.3 collective-permute-start.88
  1006.6 5.3 collective-permute-start.89
  1013.8 5.3 collective-permute-start.90
  1021.1 5.3 collective-permute-start.91
  1028.3 5.4 collective-permute-start.92
  1041.9 19.6 %reduce-scatter.17.cloned.1.call-done = bf16[32,1024]{1,0:T(8,128)(2,1)} async-done(((bf16[128,1024]{1,0:T(8,128)(2,1)}), bf16[32,1024]{1,0:T(8,128)(2,1)}) %reduce-scatter.17.cloned.1.call-update) | async-done | bytes 65552 | tf_op jit(solution)/shard_map/reduce_scatter | solution.py:132
  (558 shorter events, 202.9 us)
Async XLA Ops:
  7.2 241.3 %reduce-scatter.7.cloned.1.call-start = ((), (), s32[]{:S(2)}) async-start(), calls=%async_computation.6 | async-start | bytes 327680 | tf_op jit(solution)/shard_map/reduce_scatter | solution.py:132
  170.9 7.4 collective-permute-start.8
  227.0 289.6 %reduce-scatter.9.cloned.1.call-start = ((), (), s32[]{:S(2)}) async-start(), calls=%async_computation.7 | async-start | bytes 327680 | tf_op jit(solution)/shard_map/reduce_scatter | solution.py:132
  419.4 7.4 collective-permute-start.31
  420.3 11.9 %collective-permute-start.16 = (bf16[8,2048]{1,0:T(8,128)(2,1)S(1)}, bf16[8,2048]{1,0:T(8,128)(2,1)S(1)}, u32[]{:S(2)}, u32[]{:S(2)}) collective-permute-start(bf16[8,2048]{1,0:T(8,128)(2,1)S(1)} %reshape.547), channel_id=1, source_target_pairs={{0,1},{1,2},{2,3},{3,4},{4,5},{5,6},{6,7},{7,8},{8,9},{9,10},{10,1... | collective-permute-start | bytes 98312 | tf_op jit(solution)/shard_map/ppermute | solution.py:26
  426.8 7.4 collective-permute-start.32
  426.8 7.5 collective-permute-start.39
  432.2 7.6 collective-permute-start.24
  432.2 8.1 collective-permute-start.17
  434.3 7.5 collective-permute-start.33
  434.3 7.6 collective-permute-start.40
  449.3 7.4 collective-permute-start.42
  455.1 7.6 collective-permute-start.20
  456.6 7.6 collective-permute-start.36
  456.7 7.6 collective-permute-start.43
  461.9 7.6 collective-permute-start.28
  464.2 7.4 collective-permute-start.37
  464.3 7.5 collective-permute-start.44
  469.5 7.5 collective-permute-start.29
  470.1 7.5 collective-permute-start.22
  471.6 7.5 collective-permute-start.38
  471.7 7.6 collective-permute-start.45
  477.0 17.4 %collective-permute-start.30 = (bf16[8,2048]{1,0:T(8,128)(2,1)}, bf16[8,2048]{1,0:T(8,128)(2,1)}, u32[]{:S(2)}, u32[]{:S(2)}) collective-permute-start(bf16[8,2048]{1,0:T(8,128)(2,1)} %collective-permute-done.29), channel_id=1, source_target_pairs={{1,0},{2,1},{3,2},{4,3},{5,4},{6,5},{7,6},{8,7},{9,8},{10,9},{11,1... | collective-permute-start | bytes 98312 | tf_op jit(solution)/shard_map/ppermute | solution.py:28
  477.6 7.6 collective-permute-start.23
  500.9 38.6 %reduce-scatter.11.cloned.1.call-start = ((), (), s32[]{:S(2)}) async-start(), calls=%async_computation.8 | async-start | bytes 327680 | tf_op jit(solution)/shard_map/reduce_scatter | solution.py:132
  501.6 308.5 %reduce-scatter.13.cloned.1.call-start = ((), (), s32[]{:S(2)}) async-start(), calls=%async_computation.9 | async-start | bytes 327680 | tf_op jit(solution)/shard_map/reduce_scatter | solution.py:132
  713.0 12.3 %collective-permute-start.47 = (bf16[8,2048]{1,0:T(8,128)(2,1)S(1)}, bf16[8,2048]{1,0:T(8,128)(2,1)S(1)}, u32[]{:S(2)}, u32[]{:S(2)}) collective-permute-start(bf16[8,2048]{1,0:T(8,128)(2,1)S(1)} %reshape.556), channel_id=1, source_target_pairs={{0,1},{1,2},{2,3},{3,4},{4,5},{5,6},{6,7},{7,8},{8,9},{9,10},{10,1... | collective-permute-start | bytes 98312 | tf_op jit(solution)/shard_map/ppermute | solution.py:26
  719.4 7.8 collective-permute-start.63
  719.4 7.9 collective-permute-start.70
  725.3 7.9 collective-permute-start.48
  732.6 7.5 collective-permute-start.56
  734.6 7.5 collective-permute-start.65
  734.7 7.5 collective-permute-start.72
  742.2 7.4 collective-permute-start.66
  742.3 7.4 collective-permute-start.73
  749.6 7.4 collective-permute-start.67
  749.7 7.4 collective-permute-start.74
  757.0 7.4 collective-permute-start.68
  757.0 7.4 collective-permute-start.75
  762.3 7.5 collective-permute-start.60
  762.7 7.5 collective-permute-start.53
  764.4 7.7 collective-permute-start.69
  764.5 7.7 collective-permute-start.76
  769.8 18.2 %collective-permute-start.61 = (bf16[8,2048]{1,0:T(8,128)(2,1)}, bf16[8,2048]{1,0:T(8,128)(2,1)}, u32[]{:S(2)}, u32[]{:S(2)}) collective-permute-start(bf16[8,2048]{1,0:T(8,128)(2,1)} %collective-permute-done.60), channel_id=1, source_target_pairs={{1,0},{2,1},{3,2},{4,3},{5,4},{6,5},{7,6},{8,7},{9,8},{10,9},{11,1... | collective-permute-start | bytes 98312 | tf_op jit(solution)/shard_map/ppermute | solution.py:28
  770.3 7.7 collective-permute-start.54
  794.4 38.4 %reduce-scatter.15.cloned.1.call-start = ((), (), s32[]{:S(2)}) async-start(), calls=%async_computation.10 | async-start | bytes 327680 | tf_op jit(solution)/shard_map/reduce_scatter | solution.py:132
  795.0 266.5 %reduce-scatter.17.cloned.1.call-start = ((), (), s32[]{:S(2)}) async-start(), calls=%async_computation.11 | async-start | bytes 327680 | tf_op jit(solution)/shard_map/reduce_scatter | solution.py:132
  977.3 7.6 collective-permute-start.78
  (98 other events, 2333.7 us)
Sparse Core Ops, SparseCore 0:
  227.1 21.2 reduce-scatter.6
  501.0 15.5 reduce-scatter.8
  519.0 20.5 reduce-scatter.10
  794.6 15.4 reduce-scatter.12
  812.3 20.5 reduce-scatter.14
  1041.3 20.1 reduce-scatter.16
